TPU v7x, 128 devices: a whole 4x4x4 slice. The times are simulated.
128 devices in a mesh: group: 16 (over x, z), mp: 8 (over y, core).
Axes of the slice: x: 4, y: 4, z: 4, core: 2. Of those that a mesh axis runs over, the one named last changes fastest.
Arguments:
- stream: bfloat16 [8192, 3584], P('group', 'mp'), may hold values from -6 to 6
- prenorm_gain: float32 [3584], replicated, may hold values from 0.25 to 12
- query_weight: bfloat16 [3584, 4096], P(None, 'mp'), may hold values from -0.09375 to 0.09375
- key_weight: bfloat16 [3584, 2048], P(None, 'mp'), may hold values from -0.09375 to 0.09375
- value_weight: bfloat16 [3584, 2048], P(None, 'mp'), may hold values from -0.09375 to 0.09375
- output_weight: bfloat16 [4096, 3584], P('mp'), may hold values from -0.09375 to 0.09375
- adapter_down_rows: bfloat16 [64, 16, 3584], P('group', None, 'mp'), may hold values from -0.09375 to 0.09375
- adapter_up_query: bfloat16 [64, 16, 4096], P('group', None, 'mp'), may hold values from -1.5 to 1.5
- request_adapter: int32 [16, 4], replicated, may hold values from 0 to 63
- adapter_row_index: int32 [64], replicated, may hold values from 0 to 63, each once
- request_token_length: int32 [16, 4], replicated, may hold values from 1 to 256, 512 in all within a row
- continues_previous: int32 [16], replicated, may hold values from 0 to 1, as said below
- request_cache_block: int32 [16, 4], replicated, may hold values from 0 to 31, as said below
- cached_length: int32 [16, 4], replicated, may hold values from 1 to 256
- cached_rotated_keys: bfloat16 [32, 256, 2048], P('group', None, 'mp'), may hold values from -6 to 6
- cached_value_rows: bfloat16 [32, 256, 2048], P('group', None, 'mp'), may hold values from -6 to 6
Outputs:
- attn_out: bfloat16 [8192, 3584], P('group', 'mp')
Inputs may be any that keep to these rules, and one draw needn't show every extreme that they name: `continues_previous`: the first group has 0; some group has 1. `request_cache_block`: the owner of block b is group b // 2; blocks may be shared by requests.
All inputs are finite; a program needn't handle non-finite values.
Results may differ from a plain program's by a relative error of at most 0.017.
The roundings to bfloat16 on the way count: a program that leaves them out, or rounds other values in their place, can miss the bound.
Values may be sent and summed in bfloat16 or wider, within the bound.
No kernel may reach another device: no remote copies, remote signals or barrier semaphores. Data moves between devices by JAX's collectives and lax.ppermute only.
A program may use at most 128 MiB of HBM per device.

v0:
```python
import jax
import jax.numpy as jnp
from jax import lax
from jax.sharding import PartitionSpec as P

HEAD_WIDTH = 256
REQS = 4
adapter_scale = 2.0


def shifted(value, axis, steps):
    count = lax.axis_size(axis)
    first, last = (max(0, -steps), min(count, count - steps))
    return lax.ppermute(value, axis, [(source, source + steps) for source in range(first, last)])


def rotate(values, position, head_size):
    count = values.shape[0]
    shaped = values.reshape(count, -1, head_size)
    half = head_size // 2
    freq = 10000.0 ** (-jnp.arange(half, dtype=jnp.float32) / half)
    angle = position[:, None, None] * freq[None, None, :]
    cosine = jnp.cos(angle)
    sine = jnp.sin(angle)
    first = shaped[..., :half]
    second = shaped[..., half:]
    turned = jnp.concatenate(
        [first * cosine - second * sine, second * cosine + first * sine], axis=-1
    )
    return turned.reshape(count, -1)


def layout(lengths, cached, split_flag, prev_len, count):
    ends = jnp.cumsum(lengths)
    starts = ends - lengths
    place = jnp.arange(count, dtype=jnp.int32)
    member = ((place[:, None] >= starts[None, :]) & (place[:, None] < ends[None, :])).astype(
        jnp.int32
    )
    request = jnp.sum(member * jnp.arange(lengths.shape[0], dtype=jnp.int32)[None, :], axis=1)
    offset = place - jnp.sum(member * starts[None, :], axis=1)
    extra = jnp.where(request == 0, split_flag * prev_len, 0)
    position = jnp.sum(member * cached[None, :], axis=1) + extra + offset
    return (member, request, position.astype(jnp.float32))


def attend(
    query_vectors,
    keys,
    values,
    prev_keys,
    prev_values,
    cache_keys,
    cache_values,
    request,
    cached,
    split_flag,
    prev_len,
    head_size,
):
    count = query_vectors.shape[0]
    kv_heads = keys.shape[1] // head_size
    ratio = query_vectors.shape[1] // keys.shape[1]
    block = cache_keys.shape[1]
    slots = cache_keys.shape[0] * block
    every_key = jnp.concatenate([cache_keys.reshape(slots, -1), prev_keys, keys], 0).reshape(
        -1, kv_heads, head_size
    )
    every_value = jnp.concatenate(
        [cache_values.reshape(slots, -1), prev_values, values], 0
    ).reshape(-1, kv_heads, head_size)
    slot_req = jnp.arange(slots, dtype=jnp.int32) // block
    slot_col = jnp.arange(slots, dtype=jnp.int32) % block
    cache_ok = (request[:, None] == slot_req[None, :]) & (
        slot_col[None, :] < cached[slot_req][None, :]
    )
    place = jnp.arange(count, dtype=jnp.int32)
    prev_ok = (split_flag == 1) & (request[:, None] == 0) & (place[None, :] >= count - prev_len)
    own_ok = (request[:, None] == request[None, :]) & (place[None, :] <= place[:, None])
    allowed = jnp.concatenate([cache_ok, prev_ok, own_ok], 1)
    grouped = query_vectors.reshape(count, kv_heads, ratio, head_size)
    scores = jnp.einsum(
        "tkrd,skd->krts", grouped, every_key, preferred_element_type=jnp.float32
    ) * head_size ** (-0.5)
    scores = jnp.where(allowed[None, None], scores, jnp.float32(-1e30))
    top = jnp.max(scores, axis=-1, keepdims=True)
    weights = jnp.exp(scores - top)
    total = jnp.sum(weights, axis=-1)
    numer = jnp.einsum(
        "krts,skd->tkrd",
        weights.astype(jnp.bfloat16),
        every_value,
        preferred_element_type=jnp.float32,
    )
    result = numer / jnp.transpose(total, (2, 0, 1))[..., None]
    return result.reshape(count, -1).astype(jnp.bfloat16)


def on_device(
    stream,
    prenorm_gain,
    query_weight,
    key_weight,
    value_weight,
    output_weight,
    adapter_down_rows,
    adapter_up_query,
    request_adapter,
    adapter_row_index,
    request_token_length,
    continues_previous,
    request_cache_block,
    cached_length,
    cached_rotated_keys,
    cached_value_rows,
):
    count = stream.shape[0]
    width = stream.shape[1]
    group_at = lax.axis_index("group")
    model_at = lax.axis_index("mp")
    whole = lax.all_gather(stream, "mp", axis=1, tiled=True)
    wide = whole.astype(jnp.float32)
    normalized_input = (
        wide * lax.rsqrt(jnp.mean(wide * wide, axis=1, keepdims=True) + 1e-06) * prenorm_gain
    ).astype(jnp.bfloat16)
    normed_part = lax.dynamic_slice_in_dim(normalized_input, model_at * width, width, 1)
    before = jnp.maximum(group_at - 1, 0)
    lengths = request_token_length[group_at]
    cached = cached_length[group_at]
    split_flag = continues_previous[group_at]
    prev_len = request_token_length[before, REQS - 1]
    member, request, position = layout(lengths, cached, split_flag, prev_len, count)
    wanted = adapter_row_index[request_adapter[group_at]]
    pieces = (
        lax.all_gather(adapter_down_rows, "group", axis=0, tiled=True),
        lax.all_gather(adapter_up_query, "group", axis=0, tiled=True),
    )
    stored = jnp.arange(pieces[0].shape[0], dtype=jnp.int32)
    onehot = (wanted[:, None] == stored[None, :]).astype(jnp.bfloat16)
    new_down = jnp.einsum("rj,jkd->rkd", onehot, pieces[0], preferred_element_type=jnp.float32)
    new_up = jnp.einsum("rj,jkd->rkd", onehot, pieces[1], preferred_element_type=jnp.float32)
    chosen_down = new_down.astype(jnp.bfloat16)
    chosen_up = new_up.astype(jnp.bfloat16)
    rank_index = adapter_down_rows.shape[1]
    partial_low = jnp.einsum(
        "td,rkd->trk", normed_part, chosen_down, preferred_element_type=jnp.float32
    ).reshape(count, REQS * rank_index)
    low = lax.psum(partial_low, "mp").astype(jnp.bfloat16)
    own_columns = jnp.repeat(member, rank_index, axis=1).astype(jnp.bfloat16)
    query_update = jnp.dot(
        low * own_columns,
        chosen_up.reshape(REQS * rank_index, -1),
        preferred_element_type=jnp.float32,
    )
    query_vectors = (
        jnp.dot(normalized_input, query_weight, preferred_element_type=jnp.float32)
        + adapter_scale * query_update
    )
    query_vectors = rotate(query_vectors, position, HEAD_WIDTH).astype(jnp.bfloat16)
    keys = rotate(
        jnp.dot(normalized_input, key_weight, preferred_element_type=jnp.float32),
        position,
        HEAD_WIDTH,
    ).astype(jnp.bfloat16)
    values = jnp.dot(normalized_input, value_weight, preferred_element_type=jnp.float32).astype(
        jnp.bfloat16
    )
    prev_keys, prev_values = shifted((keys, values), "group", 1)
    blocks = request_cache_block[group_at]
    pieces = (
        lax.all_gather(cached_rotated_keys, "group", axis=0, tiled=True),
        lax.all_gather(cached_value_rows, "group", axis=0, tiled=True),
    )
    stored = jnp.arange(pieces[0].shape[0], dtype=jnp.int32)
    onehot = (blocks[:, None] == stored[None, :]).astype(jnp.bfloat16)
    new_keys = jnp.einsum("rj,jcd->rcd", onehot, pieces[0], preferred_element_type=jnp.float32)
    new_values = jnp.einsum("rj,jcd->rcd", onehot, pieces[1], preferred_element_type=jnp.float32)
    cache_keys = new_keys.astype(jnp.bfloat16)
    cache_values = new_values.astype(jnp.bfloat16)
    attended = attend(
        query_vectors,
        keys,
        values,
        prev_keys,
        prev_values,
        cache_keys,
        cache_values,
        request,
        cached,
        split_flag,
        prev_len,
        HEAD_WIDTH,
    )
    partial_out = jnp.dot(attended, output_weight, preferred_element_type=jnp.float32)
    return lax.psum_scatter(partial_out.astype(jnp.bfloat16), "mp", scatter_dimension=1, tiled=True)


def solution(mesh):
    placed = (
        P("group", "mp"),
        P(),
        P(None, "mp"),
        P(None, "mp"),
        P(None, "mp"),
        P("mp", None),
        P("group", None, "mp"),
        P("group", None, "mp"),
        P(),
        P(),
        P(),
        P(),
        P(),
        P(),
        P("group", None, "mp"),
        P("group", None, "mp"),
    )
    return jax.shard_map(
        on_device, mesh=mesh, in_specs=placed, out_specs=P("group", "mp"), check_vma=False
    )
```

profile of v0, /device:TPU:0, one launch (start us, length us, event | category | flops | bytes accessed | tf_op | source)
XLA Modules:
  0.0 254.0 jit_solution(16617972660007501374)
XLA Ops:
  6.5 0.7 all-gather.11.cloned.1.call-update
  7.3 0.0 all-gather.7.cloned.1.call-start
  7.3 0.7 all-gather.7.cloned.1.call-update
  8.0 0.0 all-gather.5.cloned.1.call-start
  8.1 0.7 all-gather.5.cloned.1.call-update
  8.7 0.0 all-gather.9.cloned.1.call-start
  8.8 0.5 all-gather.9.cloned.1.call-update
  9.3 0.0 reduce-scatter.2.cloned.1.call-start
  9.4 1.3 constant_dynamic-slice_fusion.2
  10.7 0.9 dynamic-slice_reduce_fusion
  11.6 0.1 copy.61
  11.7 0.2 reduce-window.4
  11.9 0.9 fusion.79
  12.8 0.6 fusion.81
  13.4 26.9 %all_gather.18 = bf16[64,16,448]{2,1,0:T(8,128)(2,1)S(1)} all-gather(bf16[4,16,448]{2,1,0:T(8,128)(2,1)} %param.22), channel_id=1, replica_groups=mesh['group'=16,'mp'=8] {'group'}, dimensions={0}, use_global_device_ids=true | all-gather | bytes 974848 | tf_op jit(solution)/shard_map/all_gather | solution.py:135
  40.9 2.6 %compare_select_fusion.1 = s32[1024,1]{0,1:T(1,128)S(1)} fusion(s32[]{:T(128)} %bitcast.7, s32[]{:T(128)} %bitcast.8, s32[]{:T(128)} %bitcast.10, s32[]{:T(128)} %bitcast.9), kind=kLoop, calls=%fused_computation.71 | loop fusion | flops 17408 | bytes 4112 | tf_op jit(solution)/shard_map/gather | solution.py:75
  43.5 1.2 dynamic_slice.24
  46.8 0.9 dynamic-slice_reduce_fusion.1
  47.6 1.3 gather_fusion
  48.9 0.1 select_reduce_fusion.2
  49.0 0.1 convert_convert_fusion
  49.1 0.2 broadcast_and_fusion
  49.3 0.2 fusion.35
  49.5 1.8 multiply_cosine_fusion
  51.4 0.8 compare_and_fusion
  52.2 1.2 convolution_convert_fusion.3
  53.4 0.4 pad_add_fusion
  53.8 1.2 all-gather.11.cloned.1.call-done
  54.9 2.4 convolution_convert_fusion.2
  57.4 28.5 %all-gather.7.cloned.1.call-done = bf16[512,3584]{0,1:T(8,128)(2,1)} async-done(((bf16[512,448]{0,1:T(8,128)(2,1)}), bf16[512,3584]{0,1:T(8,128)(2,1)}) %all-gather.7.cloned.1.call-update) | async-done | bytes 3670032 | tf_op jit(solution)/shard_map/all_gather | solution.py:121
  85.8 3.0 %fusion.2 = f32[512]{0:T(512)S(1)} fusion(bf16[512,3584]{0,1:T(8,128)(2,1)} %all-gather.7.cloned.1.call-done), kind=kLoop, calls=%fused_computation.7 | loop fusion | flops 5504512 | bytes 3672064 | tf_op jit(solution)/shard_map/reduce_sum | solution.py:124
  88.9 0.1 copy-done.1
  89.0 1.6 fusion.4
  90.6 1.8 copy-done.2
  92.4 1.9 convolution_convert_fusion.1
  94.3 1.8 copy.47
  96.1 4.2 %collective-permute-start = (bf16[512,256]{1,0:T(8,128)(2,1)}, bf16[512,256]{1,0:T(8,128)(2,1)}, u32[]{:S(2)}, u32[]{:S(2)}) collective-permute-start(bf16[512,256]{1,0:T(8,128)(2,1)} %convolution_convert_fusion.1), channel_id=1, source_target_pairs={{0,8},{8,16},{16,24},{24,32},{32,40},{40,48},{48,56},{56,64},{64,7... | collective-permute-start | bytes 786440 | tf_op jit(solution)/shard_map/ppermute | solution.py:14
  100.2 3.8 %convolution_bitcast_fusion = f32[512,1,256]{0,2,1:T(8,128)S(1)} fusion(bf16[512,3584]{0,1:T(8,128)(2,1)} %copy-done.2, bf16[3584,256]{1,0:T(8,128)(2,1)} %param.19), kind=kOutput, calls=%fused_computation.26 | convolution fusion | flops 939524096 | bytes 6029312 | tf_op jit(solution)/shard_map/dot_general | solution.py:161
  104.0 1.2 fusion.49
  105.2 0.7 maximum_bitcast_fusion.6
  105.9 1.8 copy.52
  107.7 3.4 %collective-permute-start.1 = (bf16[512,256]{0,1:T(8,128)(2,1)}, bf16[512,256]{0,1:T(8,128)(2,1)}, u32[]{:S(2)}, u32[]{:S(2)}) collective-permute-start(bf16[512,256]{0,1:T(8,128)(2,1)} %maximum_bitcast_fusion.6), channel_id=1, source_target_pairs={{0,8},{8,16},{16,24},{24,32},{32,40},{40,48},{48,56},{56,64},{64,7... | collective-permute-start | bytes 786440 | tf_op jit(solution)/shard_map/ppermute | solution.py:14
  111.1 1.2 fusion.41
  112.3 26.0 %all-reduce.1 = bf16[512,64]{0,1:T(8,128)(2,1)S(1)} all-reduce(f32[512,64]{0,1:T(8,128)S(1)} %bitcast.101), channel_id=1, replica_groups=mesh['group'=16,'mp'=8] {'mp'}, use_global_device_ids=true, to_apply=%region_5.6 | all-reduce | flops 32768 | bytes 196608 | tf_op jit(solution)/shard_map/psum | solution.py:148
  138.4 5.3 %fusion.82 = f32[512,512]{0,1:T(8,128)S(1)} fusion(bf16[512,3584]{0,1:T(8,128)(2,1)} %copy-done.2, bf16[3584,512]{1,0:T(8,128)(2,1)} %param.18), kind=kOutput, calls=%fused_computation.129 | convolution fusion | flops 1879048192 | bytes 8388608 | tf_op jit(solution)/shard_map/dot_general | solution.py:156
  143.7 0.3 fusion.17
  144.0 1.1 fusion.80
  145.1 1.2 copy.63
  146.4 2.1 copy.62
  148.5 2.2 subtract_convert_fusion
  150.6 1.8 copy.46
  152.5 1.8 copy.51
  154.3 4.6 %fusion.18 = bf16[4,256,256]{2,0,1:T(4,128)(2,1)S(1)} fusion(bf16[32,256,256]{2,1,0:T(8,128)(2,1)} %all-gather.5.cloned.1.call-done, s32[4]{0:T(128)S(1)} %dynamic-slice_reduce_fusion.1), kind=kOutput, calls=%fused_computation.24 | convolution fusion | flops 17039488 | bytes 4718608 | tf_op jit(solution)/shard_map/rj,jcd->rcd/dot_general | solution.py:177
  158.9 0.1 copy.44
  159.0 1.0 copy.45
  160.0 35.3 %all-gather.9.cloned.1.call-done = bf16[32,256,256]{2,1,0:T(8,128)(2,1)} async-done(((bf16[2,256,256]{2,1,0:T(8,128)(2,1)}), bf16[32,256,256]{2,1,0:T(8,128)(2,1)}) %all-gather.9.cloned.1.call-update) | async-done | bytes 4194320 | tf_op jit(solution)/shard_map/all_gather | solution.py:171
  195.3 4.7 %fusion.21 = bf16[4,256,256]{2,0,1:T(4,128)(2,1)S(1)} fusion(bf16[32,256,256]{2,1,0:T(8,128)(2,1)} %all-gather.9.cloned.1.call-done, s32[4]{0:T(128)S(1)} %dynamic-slice_reduce_fusion.1), kind=kOutput, calls=%fused_computation.25 | convolution fusion | flops 17039488 | bytes 4718608 | tf_op jit(solution)/shard_map/rj,jcd->rcd/dot_general | solution.py:176
  200.0 0.1 copy.50
  200.1 1.8 fusion.5
  201.9 2.2 fusion
  204.2 2.8 %divide_convert_fusion = bf16[512,1,2,256]{0,3,2,1:T(8,128)(2,1)S(1)} fusion(f32[2048,512,2]{1,0,2:T(8,128)S(1)} %get-tuple-element.25, f32[2,512]{1,0:T(2,128)S(1)} %get-tuple-element.24, pred[512,2048]{0,1:T(8,128)(4,1)S(1)} %pad_add_fusion, bf16[512,256]{0,1:T(8,128)(2,1)S(1)} %copy-done.4, bf16[512,256]{0,1:T(8,128)(2,1)S(1)} %copy-done.6, ...), kind=kOutput, calls=%fused_computation.43 | convolution fusion | flops 1085800448 | bytes 11018240 | tf_op jit(solution)/shard_map/krts,skd->tkrd/dot_general | solution.py:89
  207.0 3.9 %convolution_convert_fusion = bf16[512,3584]{0,1:T(8,128)(2,1)} fusion(bf16[512,512]{0,1:T(8,128)(2,1)S(1)} %bitcast.107, bf16[512,3584]{1,0:T(8,128)(2,1)S(1)} %copy-done.11), kind=kOutput, calls=%fused_computation.11 | convolution fusion | flops 1880883200 | bytes 7864320 | tf_op jit(solution)/shard_map/dot_general | solution.py:194
  210.9 0.0 reduce-scatter.2.cloned.1.call-update
  210.9 36.5 %reduce-scatter.2.cloned.1.call-done = bf16[512,448]{0,1:T(8,128)(2,1)} async-done(((bf16[512,3584]{0,1:T(8,128)(2,1)}), bf16[512,448]{0,1:T(8,128)(2,1)}) %reduce-scatter.2.cloned.1.call-update) | async-done | bytes 458768 | tf_op jit(solution)/shard_map/reduce_scatter | solution.py:195
  (38 shorter events, 0.2 us)
Async XLA Ops:
  6.5 85.8 %copy-start = (bf16[3584,256]{1,0:T(8,128)(2,1)S(1)}, bf16[3584,256]{1,0:T(8,128)(2,1)}, u32[]{:S(2)}) copy-start(bf16[3584,256]{1,0:T(8,128)(2,1)} %param.20) | copy-start | bytes 5505028
  6.5 48.4 %all-gather.11.cloned.1.call-start = ((), (), s32[]{:S(2)}) async-start(), calls=%async_computation.4 | async-start | bytes 1114112 | tf_op jit(solution)/shard_map/all_gather | solution.py:136
  7.3 78.6 %all-gather.7.cloned.1.call-start = ((), (), s32[]{:S(2)}) async-start(), calls=%async_computation.2 | async-start | bytes 4128768 | tf_op jit(solution)/shard_map/all_gather | solution.py:121
  8.0 146.3 %all-gather.5.cloned.1.call-start = ((), (), s32[]{:S(2)}) async-start(), calls=%async_computation.1 | async-start | bytes 4456448 | tf_op jit(solution)/shard_map/all_gather | solution.py:172
  8.7 186.5 %all-gather.9.cloned.1.call-start = ((), (), s32[]{:S(2)}) async-start(), calls=%async_computation.3 | async-start | bytes 4456448 | tf_op jit(solution)/shard_map/all_gather | solution.py:171
  9.3 238.1 %reduce-scatter.2.cloned.1.call-start = ((), (), s32[]{:S(2)}) async-start(), calls=%async_computation.5 | async-start | bytes 4128768 | tf_op jit(solution)/shard_map/reduce_scatter | solution.py:195
  53.4 35.5 %copy-start.10 = (f32[3584]{0:T(1024)S(1)}, f32[3584]{0:T(1024)}, u32[]{:S(2)}) copy-start(f32[3584]{0:T(1024)} %param.17) | copy-start | bytes 43012
  85.8 3.1 %copy-start.1 = (bf16[512,3584]{0,1:T(8,128)(2,1)S(1)}, bf16[512,3584]{0,1:T(8,128)(2,1)}, u32[]{:S(2)}) copy-start(bf16[512,3584]{0,1:T(8,128)(2,1)} %all-gather.7.cloned.1.call-done) | copy-start | bytes 11010052
  90.5 1.8 copy-start.2
  96.1 54.6 %collective-permute-start = (bf16[512,256]{1,0:T(8,128)(2,1)}, bf16[512,256]{1,0:T(8,128)(2,1)}, u32[]{:S(2)}, u32[]{:S(2)}) collective-permute-start(bf16[512,256]{1,0:T(8,128)(2,1)} %convolution_convert_fusion.1), channel_id=1, source_target_pairs={{0,8},{8,16},{16,24},{24,32},{32,40},{40,48},{48,56},{56,64},{64,7... | collective-permute-start | bytes 786440 | tf_op jit(solution)/shard_map/ppermute | solution.py:14
  107.7 44.8 %collective-permute-start.1 = (bf16[512,256]{0,1:T(8,128)(2,1)}, bf16[512,256]{0,1:T(8,128)(2,1)}, u32[]{:S(2)}, u32[]{:S(2)}) collective-permute-start(bf16[512,256]{0,1:T(8,128)(2,1)} %maximum_bitcast_fusion.6), channel_id=1, source_target_pairs={{0,8},{8,16},{16,24},{24,32},{32,40},{40,48},{48,56},{56,64},{64,7... | collective-permute-start | bytes 786440 | tf_op jit(solution)/shard_map/ppermute | solution.py:14
  160.0 40.1 %copy-start.5 = (bf16[512,256]{1,0:T(8,128)(2,1)S(1)}, bf16[512,256]{1,0:T(8,128)(2,1)}, u32[]{:S(2)}) copy-start(bf16[512,256]{1,0:T(8,128)(2,1)} %copy.52) | copy-start | bytes 786436
  160.0 40.1 %copy-start.7 = (bf16[512,256]{1,0:T(8,128)(2,1)S(1)}, bf16[512,256]{1,0:T(8,128)(2,1)}, u32[]{:S(2)}) copy-start(bf16[512,256]{1,0:T(8,128)(2,1)} %copy.51) | copy-start | bytes 786436
  195.3 4.8 %copy-start.8 = (bf16[512,2,128]{2,0,1:T(8,128)(2,1)S(1)}, bf16[512,2,128]{2,0,1:T(8,128)(2,1)}, u32[]{:S(2)}) copy-start(bf16[512,2,128]{2,0,1:T(8,128)(2,1)} %get-tuple-element.12) | copy-start | bytes 786436
  195.3 4.8 %copy-start.9 = (bf16[512,2,128]{2,0,1:T(8,128)(2,1)S(1)}, bf16[512,2,128]{2,0,1:T(8,128)(2,1)}, u32[]{:S(2)}) copy-start(bf16[512,2,128]{2,0,1:T(8,128)(2,1)} %get-tuple-element.13) | copy-start | bytes 786436
  201.9 2.2 copy-start.3
  201.9 2.2 copy-start.4
  201.9 2.2 copy-start.6
  204.2 2.8 %copy-start.11 = (bf16[512,3584]{1,0:T(8,128)(2,1)S(1)}, bf16[512,3584]{1,0:T(8,128)(2,1)}, u32[]{:S(2)}) copy-start(bf16[512,3584]{1,0:T(8,128)(2,1)} %param.21) | copy-start | bytes 11010052
Sparse Core Ops, SparseCore 0:
  9.5 45.3 all-gather.10
  56.6 29.1 all-gather.6
  88.0 53.9 all-gather.4
  144.0 51.2 all-gather.8
  211.0 36.3 reduce-scatter.1
where the time goes:
time: 255 us; the launch traced here: 254 us
  waiting for transfers between devices  104 us (41%)
  blocking collectives  52.9 us (21%)
  matrix products  33.9 us (13%)
  local copies, waits for them, and re-layouts  21.9 us (9%)
  other arithmetic  17.3 us (7%)
  between operations  16.1 us (6%)
  starting transfers between devices  7.77 us (3%)
    reduce_scatter x1, waiting for transfers between devices, on_device(): lax.psum_scatter(partial_out.astype(jnp.bfloat16), 'mp', scatter_dimensio...  36.5 us
    all_gather x1, waiting for transfers between devices, on_device(): lax.all_gather(cached_rotated_keys, 'group', axis=0, tiled=True)  35.3 us
    all_gather x1, waiting for transfers between devices, on_device(): whole = lax.all_gather(stream, 'mp', axis=1, tiled=True)  28.5 us
    all_gather x1, blocking collectives, on_device(): lax.all_gather(adapter_down_rows, 'group', axis=0, tiled=True)  26.9 us
    psum x1, blocking collectives, on_device(): low = lax.psum(partial_low, 'mp').astype(jnp.bfloat16)  26 us
    ppermute x2, starting transfers between devices, shifted(): lax.ppermute(value, axis, [(source, source + steps) for source in range(f...  7.62 us
    unnamed x27, local copies, waits for them, and re-layouts  5.37 us
    dot_general x1, matrix products, on_device(): jnp.dot(normalized_input, query_weight, preferred_element_type=jnp.float32)  5.26 us
  transfers between devices with their start and end apart: 7, of which 4 were waited for; matrix products, arithmetic and copies ran while one was open for 22% of the time, Pallas kernels for 0%

commit v1 on v0

--- a/solution.py
+++ b/solution.py
@@ -145,7 +145,7 @@
     partial_low = jnp.einsum(
         "td,rkd->trk", normed_part, chosen_down, preferred_element_type=jnp.float32
     ).reshape(count, REQS * rank_index)
-    low = lax.psum(partial_low, "mp").astype(jnp.bfloat16)
+    low = jnp.sum(lax.all_gather(partial_low, "mp"), axis=0).astype(jnp.bfloat16)
     own_columns = jnp.repeat(member, rank_index, axis=1).astype(jnp.bfloat16)
     query_update = jnp.dot(
         low * own_columns,

time: 255 us -> 286 us (1.12)
  waiting for transfers between devices: 104 us -> 163 us
  blocking collectives: 52.9 us -> 27.6 us
  local copies, waits for them, and re-layouts: 21.9 us -> 18.8 us
    all_gather x1, waiting for transfers between devices: 0.01 us -> 27.5 us  [on_device(): lax.all_gather(cached_value_rows, 'group', axis=0, tiled=True)]
    psum x1 -> x0, blocking collectives: 26 us -> none  [on_device(): low = lax.psum(partial_low, 'mp').astype(jnp.bfloat16)]
    all_gather x0 -> x1, waiting for transfers between devices: none -> 19.1 us  [on_device(): lax.all_gather(partial_low, 'mp')]
    all_gather x1, waiting for transfers between devices: 35.3 us -> 47.6 us  [on_device(): lax.all_gather(cached_rotated_keys, 'group', axis=0, tiled=True)]
  transfers between devices with their start and end apart: 7 -> 8, of which waited for: 4 -> 6; matrix products, arithmetic and copies ran while one was open for 22% -> 17% of each run, Pallas kernels for 0% -> 0%
where the time goes in v1:
time: 286 us; the launch traced here: 285 us
  waiting for transfers between devices  163 us (57%)
  matrix products  34.6 us (12%)
  blocking collectives  27.6 us (10%)
  local copies, waits for them, and re-layouts  18.8 us (7%)
  other arithmetic  16.8 us (6%)
  between operations  16.3 us (6%)
  starting transfers between devices  7.86 us (3%)
    all_gather x1, waiting for transfers between devices, on_device(): lax.all_gather(cached_rotated_keys, 'group', axis=0, tiled=True)  47.6 us
    reduce_scatter x1, waiting for transfers between devices, on_device(): lax.psum_scatter(partial_out.astype(jnp.bfloat16), 'mp', scatter_dimensio...  36.9 us
    all_gather x1, waiting for transfers between devices, on_device(): whole = lax.all_gather(stream, 'mp', axis=1, tiled=True)  28.4 us
    all_gather x1, blocking collectives, on_device(): lax.all_gather(adapter_down_rows, 'group', axis=0, tiled=True)  27.6 us
    all_gather x1, waiting for transfers between devices, on_device(): lax.all_gather(cached_value_rows, 'group', axis=0, tiled=True)  27.5 us
    all_gather x1, waiting for transfers between devices, on_device(): lax.all_gather(partial_low, 'mp')  19.1 us
    ppermute x2, starting transfers between devices, shifted(): lax.ppermute(value, axis, [(source, source + steps) for source in range(f...  7.66 us
  transfers between devices with their start and end apart: 8, of which 6 were waited for; matrix products, arithmetic and copies ran while one was open for 17% of the time, Pallas kernels for 0%

profile of v1, /device:TPU:0, one launch (start us, length us, event | category | flops | bytes accessed | tf_op | source)
XLA Modules:
  0.0 284.7 jit_solution(6269163223299927176)
XLA Ops:
  6.5 0.7 all-gather.14.cloned.1.call-update
  7.3 0.0 all-gather.8.cloned.1.call-start
  7.3 0.7 all-gather.8.cloned.1.call-update
  8.0 0.0 all-gather.6.cloned.1.call-start
  8.1 0.7 all-gather.6.cloned.1.call-update
  8.7 0.0 all-gather.10.cloned.1.call-start
  8.8 0.5 all-gather.10.cloned.1.call-update
  9.3 0.0 all-gather.12.cloned.1.call-start
  9.4 1.3 constant_dynamic-slice_fusion.2
  11.3 1.2 dynamic_slice.24
  14.5 0.9 dynamic-slice_reduce_fusion.1
  15.4 0.9 dynamic-slice_reduce_fusion
  16.2 0.1 copy.58
  16.3 0.2 reduce-window.4
  16.5 1.3 gather_fusion
  17.9 0.9 fusion.83
  18.7 0.6 fusion.85
  19.3 2.6 compare_select_fusion.1
  21.9 0.1 select_reduce_fusion.2
  22.0 27.6 %all_gather.21 = bf16[64,16,448]{2,1,0:T(8,128)(2,1)S(1)} all-gather(bf16[4,16,448]{2,1,0:T(8,128)(2,1)} %param.22), channel_id=1, replica_groups=mesh['group'=16,'mp'=8] {'group'}, dimensions={0}, use_global_device_ids=true | all-gather | bytes 974848 | tf_op jit(solution)/shard_map/all_gather | solution.py:135
  49.6 0.1 convert_convert_fusion
  49.7 0.2 broadcast_and_fusion
  49.9 0.2 fusion.36
  50.1 1.8 multiply_cosine_fusion
  51.9 0.8 compare_and_fusion
  52.7 1.2 convolution_convert_fusion.3
  54.0 0.4 pad_add_fusion
  54.3 0.6 all-gather.14.cloned.1.call-done
  55.0 2.4 convolution_convert_fusion.2
  57.4 28.4 %all-gather.8.cloned.1.call-done = bf16[512,3584]{0,1:T(8,128)(2,1)} async-done(((bf16[512,448]{0,1:T(8,128)(2,1)}), bf16[512,3584]{0,1:T(8,128)(2,1)}) %all-gather.8.cloned.1.call-update) | async-done | bytes 3670032 | tf_op jit(solution)/shard_map/all_gather | solution.py:121
  85.8 3.0 %fusion.2 = f32[512]{0:T(512)S(1)} fusion(bf16[512,3584]{0,1:T(8,128)(2,1)} %all-gather.8.cloned.1.call-done), kind=kLoop, calls=%fused_computation.7 | loop fusion | flops 5504512 | bytes 3672064 | tf_op jit(solution)/shard_map/reduce_sum | solution.py:124
  88.8 0.1 copy-done.1
  88.9 1.6 fusion.4
  90.5 1.9 convolution_convert_fusion.1
  92.4 3.5 %collective-permute-start = (bf16[512,256]{1,0:T(8,128)(2,1)}, bf16[512,256]{1,0:T(8,128)(2,1)S(1)}, u32[]{:S(2)}, u32[]{:S(2)}) collective-permute-start(bf16[512,256]{1,0:T(8,128)(2,1)} %convolution_convert_fusion.1), channel_id=1, source_target_pairs={{0,8},{8,16},{16,24},{24,32},{32,40},{40,48},{48,56},{56,64},{64,7... | collective-permute-start | bytes 786440 | tf_op jit(solution)/shard_map/ppermute | solution.py:14
  95.9 0.9 fusion.42
  96.8 0.0 reduce-scatter.2.cloned.1.call-start
  96.8 4.1 %convolution_bitcast_fusion.1 = f32[512,1,256]{0,2,1:T(8,128)S(1)} fusion(bf16[512,3584]{0,1:T(8,128)(2,1)} %copy-done.2, bf16[3584,256]{1,0:T(8,128)(2,1)} %param.19), kind=kOutput, calls=%fused_computation.27 | convolution fusion | flops 939524096 | bytes 6029312 | tf_op jit(solution)/shard_map/dot_general | solution.py:161
  100.9 1.2 fusion.50
  102.1 4.2 %collective-permute-start.1 = (bf16[512,256]{0,1:T(8,128)(2,1)S(1)}, bf16[512,256]{0,1:T(8,128)(2,1)}, u32[]{:S(2)}, u32[]{:S(2)}) collective-permute-start(bf16[512,256]{0,1:T(8,128)(2,1)S(1)} %maximum_bitcast_fusion.6), channel_id=1, source_target_pairs={{0,8},{8,16},{16,24},{24,32},{32,40},{40,48},{48,56},{56,64},{64,7... | collective-permute-start | bytes 786440 | tf_op jit(solution)/shard_map/ppermute | solution.py:14
  106.3 3.1 %fusion.86 = f32[512,512]{0,1:T(8,128)} fusion(bf16[512,3584]{0,1:T(8,128)(2,1)S(1)} %copy-done.3, bf16[3584,512]{1,0:T(8,128)(2,1)S(1)} %copy-done.8), kind=kOutput, calls=%fused_computation.132 | convolution fusion | flops 1879048192 | bytes 8388608 | tf_op jit(solution)/shard_map/dot_general | solution.py:156
  109.5 1.8 copy.44
  111.3 0.8 copy.49
  112.1 0.8 copy.43
  113.0 1.8 copy.48
  114.8 27.5 %all-gather.6.cloned.1.call-done = bf16[32,256,256]{2,1,0:T(8,128)(2,1)} async-done(((bf16[2,256,256]{2,1,0:T(8,128)(2,1)}), bf16[32,256,256]{2,1,0:T(8,128)(2,1)}) %all-gather.6.cloned.1.call-update) | async-done | bytes 4194320 | tf_op jit(solution)/shard_map/all_gather | solution.py:172
  142.3 4.6 %fusion.19 = bf16[4,256,256]{2,0,1:T(4,128)(2,1)S(1)} fusion(bf16[32,256,256]{2,1,0:T(8,128)(2,1)} %all-gather.6.cloned.1.call-done, s32[4]{0:T(128)S(1)} %dynamic-slice_reduce_fusion.1), kind=kOutput, calls=%fused_computation.25 | convolution fusion | flops 17039488 | bytes 4718608 | tf_op jit(solution)/shard_map/rj,jcd->rcd/dot_general | solution.py:177
  146.9 0.1 copy.41
  147.0 1.0 copy.42
  148.0 47.6 %all-gather.10.cloned.1.call-done = bf16[32,256,256]{2,1,0:T(8,128)(2,1)} async-done(((bf16[2,256,256]{2,1,0:T(8,128)(2,1)}), bf16[32,256,256]{2,1,0:T(8,128)(2,1)}) %all-gather.10.cloned.1.call-update) | async-done | bytes 4194320 | tf_op jit(solution)/shard_map/all_gather | solution.py:171
  195.6 4.6 %fusion.22 = bf16[4,256,256]{2,0,1:T(4,128)(2,1)S(1)} fusion(bf16[32,256,256]{2,1,0:T(8,128)(2,1)} %all-gather.10.cloned.1.call-done, s32[4]{0:T(128)S(1)} %dynamic-slice_reduce_fusion.1), kind=kOutput, calls=%fused_computation.26 | convolution fusion | flops 17039488 | bytes 4718608 | tf_op jit(solution)/shard_map/rj,jcd->rcd/dot_general | solution.py:176
  200.2 0.8 copy.47
  201.1 19.1 %all-gather.12.cloned.1.call-done = f32[8,512,64]{1,2,0:T(8,128)} async-done(((f32[1,512,64]{1,2,0:T(8,128)}), f32[8,512,64]{1,2,0:T(8,128)}) %all-gather.12.cloned.1.call-update) | async-done | bytes 1048592 | tf_op jit(solution)/shard_map/all_gather | solution.py:148
  220.1 1.3 reduce_sum.60
  221.4 1.6 fusion.18
  223.0 1.1 fusion.84
  224.1 1.2 copy.60
  225.3 2.0 copy.59
  227.4 1.3 subtract_convert_fusion
  228.7 3.5 %fusion.5 = (f32[2,512]{1,0:T(2,128)S(1)}, f32[2048,512,2]{1,0,2:T(8,128)S(1)}) fusion(pred[512,2048]{0,1:T(8,128)(4,1)S(1)} %pad_add_fusion, bf16[512,2,128]{2,0,1:T(8,128)(2,1)S(1)} %get-tuple-element.13, bf16[512,2,128]{2,0,1:T(8,128)(2,1)S(1)} %get-tuple-element.12, bf16[512,256]{1,0:T(8,128)(2,1)} %copy.49, bf16[512,256]{1,0:T(8,128)(2,1)} %copy.48, ...), kind=kOutput, calls=%fused_computation.10 | convolution fusion | flops 1084226560 | bytes 11014144 | tf_op jit(solution)/shard_map/tkrd,skd->krts/dot_general | solution.py:82
  232.3 2.0 fusion
  234.3 2.8 divide_convert_fusion
  237.1 3.9 %convolution_convert_fusion = bf16[512,3584]{0,1:T(8,128)(2,1)} fusion(bf16[512,512]{0,1:T(8,128)(2,1)S(1)} %bitcast.109, bf16[512,3584]{1,0:T(8,128)(2,1)S(1)} %copy-done.9), kind=kOutput, calls=%fused_computation.11 | convolution fusion | flops 1880883200 | bytes 7864320 | tf_op jit(solution)/shard_map/dot_general | solution.py:194
  241.0 36.9 %reduce-scatter.2.cloned.1.call-done = bf16[512,448]{0,1:T(8,128)(2,1)} async-done(((bf16[512,3584]{0,1:T(8,128)(2,1)}), bf16[512,448]{0,1:T(8,128)(2,1)}) %reduce-scatter.2.cloned.1.call-update) | async-done | bytes 458768 | tf_op jit(solution)/shard_map/reduce_scatter | solution.py:195
  (35 shorter events, 0.2 us)
Async XLA Ops:
  6.5 84.0 %copy-start = (bf16[3584,256]{1,0:T(8,128)(2,1)S(1)}, bf16[3584,256]{1,0:T(8,128)(2,1)}, u32[]{:S(2)}) copy-start(bf16[3584,256]{1,0:T(8,128)(2,1)} %param.20) | copy-start | bytes 5505028
  6.5 48.4 %all-gather.14.cloned.1.call-start = ((), (), s32[]{:S(2)}) async-start(), calls=%async_computation.5 | async-start | bytes 1114112 | tf_op jit(solution)/shard_map/all_gather | solution.py:136
  7.3 78.5 %all-gather.8.cloned.1.call-start = ((), (), s32[]{:S(2)}) async-start(), calls=%async_computation.2 | async-start | bytes 4128768 | tf_op jit(solution)/shard_map/all_gather | solution.py:121
  8.0 134.3 %all-gather.6.cloned.1.call-start = ((), (), s32[]{:S(2)}) async-start(), calls=%async_computation.1 | async-start | bytes 4456448 | tf_op jit(solution)/shard_map/all_gather | solution.py:172
  8.7 186.8 %all-gather.10.cloned.1.call-start = ((), (), s32[]{:S(2)}) async-start(), calls=%async_computation.3 | async-start | bytes 4456448 | tf_op jit(solution)/shard_map/all_gather | solution.py:171
  9.3 210.8 %all-gather.12.cloned.1.call-start = ((), (), s32[]{:S(2)}) async-start(), calls=%async_computation.4 | async-start | bytes 1179648 | tf_op jit(solution)/shard_map/all_gather | solution.py:148
  54.0 34.9 %copy-start.7 = (f32[3584]{0:T(1024)S(1)}, f32[3584]{0:T(1024)}, u32[]{:S(2)}) copy-start(f32[3584]{0:T(1024)} %param.17) | copy-start | bytes 43012
  85.8 3.1 %copy-start.1 = (bf16[512,3584]{0,1:T(8,128)(2,1)S(1)}, bf16[512,3584]{0,1:T(8,128)(2,1)}, u32[]{:S(2)}) copy-start(bf16[512,3584]{0,1:T(8,128)(2,1)} %all-gather.8.cloned.1.call-done) | copy-start | bytes 11010052
  90.5 5.4 %copy-start.2 = (bf16[512,3584]{0,1:T(8,128)(2,1)}, bf16[512,3584]{0,1:T(8,128)(2,1)S(1)}, u32[]{:S(2)}) copy-start(bf16[512,3584]{0,1:T(8,128)(2,1)S(1)} %fusion.4) | copy-start | bytes 11010052
  92.4 19.7 %collective-permute-start = (bf16[512,256]{1,0:T(8,128)(2,1)}, bf16[512,256]{1,0:T(8,128)(2,1)S(1)}, u32[]{:S(2)}, u32[]{:S(2)}) collective-permute-start(bf16[512,256]{1,0:T(8,128)(2,1)} %convolution_convert_fusion.1), channel_id=1, source_target_pairs={{0,8},{8,16},{16,24},{24,32},{32,40},{40,48},{48,56},{56,64},{64,7... | collective-permute-start | bytes 786440 | tf_op jit(solution)/shard_map/ppermute | solution.py:14
  96.8 181.1 %reduce-scatter.2.cloned.1.call-start = ((), (), s32[]{:S(2)}) async-start(), calls=%async_computation.6 | async-start | bytes 4128768 | tf_op jit(solution)/shard_map/reduce_scatter | solution.py:195
  96.8 9.5 %copy-start.3 = (bf16[512,3584]{0,1:T(8,128)(2,1)S(1)}, bf16[512,3584]{0,1:T(8,128)(2,1)}, u32[]{:S(2)}) copy-start(bf16[512,3584]{0,1:T(8,128)(2,1)} %copy-done.2) | copy-start | bytes 11010052
  96.8 9.5 %copy-start.8 = (bf16[3584,512]{1,0:T(8,128)(2,1)S(1)}, bf16[3584,512]{1,0:T(8,128)(2,1)}, u32[]{:S(2)}) copy-start(bf16[3584,512]{1,0:T(8,128)(2,1)} %param.18) | copy-start | bytes 11010052
  102.1 10.8 %collective-permute-start.1 = (bf16[512,256]{0,1:T(8,128)(2,1)S(1)}, bf16[512,256]{0,1:T(8,128)(2,1)}, u32[]{:S(2)}, u32[]{:S(2)}) collective-permute-start(bf16[512,256]{0,1:T(8,128)(2,1)S(1)} %maximum_bitcast_fusion.6), channel_id=1, source_target_pairs={{0,8},{8,16},{16,24},{24,32},{32,40},{40,48},{48,56},{56,64},{64,7... | collective-permute-start | bytes 786440 | tf_op jit(solution)/shard_map/ppermute | solution.py:14
  232.2 2.0 copy-start.4
  232.2 2.0 copy-start.5
  232.2 2.0 copy-start.6
  234.3 2.8 copy-start.9
Sparse Core Ops, SparseCore 0:
  9.5 45.4 all-gather.13
  56.6 29.1 all-gather.7
  87.9 54.3 all-gather.5
  144.3 51.2 all-gather.9
  197.1 22.9 all-gather.11
  241.1 36.7 reduce-scatter.1
